TPU v7x, 128 devices: a whole 4x4x4 slice. The times are simulated.
128 devices in a mesh: grp: 8 (over y, core), shard: 16 (over z, x).
Axes of the slice: x: 4, y: 4, z: 4, core: 2. Of those that a mesh axis runs over, the one named last changes fastest.
Arguments:
- tokens: bfloat16 [65536, 2560], P(('grp', 'shard')), may hold values from -6 to 6
- gain: float32 [2560], replicated, may hold values from 0.25 to 1.75
- w_qkv: bfloat16 [2560, 3072], P(None, 'shard'), may hold values from -1 to 1
- prefix_kv: bfloat16 [8, 2048, 512], P('grp', 'shard'), may hold values from -6 to 6
- prefix_owner: int32 [8], P('grp'), may hold values from 0 to 7, as said below
- suffix_len: int32 [8, 16], P('grp', 'shard'), may hold values from 1 to 512, 5120 in all within a row
- slots: int32 [8, 8192], P('grp', 'shard'), may hold values from 0 to 8191, as said below
Outputs:
- attended: bfloat16 [65536, 2560], P(('grp', 'shard'))
Inputs may be any that keep to these rules, and one draw needn't show every extreme that they name: In each group the slots are a permutation of 0 to 8191; in each aligned run of 512 entries the k-th block of 32 entries holds slots k * 512 to (k + 1) * 512 - 1. `suffix_len`: each group's lengths sum to 5120 and one of them equals 512. `prefix_owner`: each entry names one of the 8 caches; several groups may name the same one.
All inputs are finite; a program needn't handle non-finite values.
Results may differ from a plain program's by a relative error of at most 0.0069.
Values may be sent and summed in bfloat16 or wider, within the bound.
No kernel may reach another device: no remote copies, remote signals or barrier semaphores. Data moves between devices by JAX's collectives and lax.ppermute only.
A program may use at most 128 MiB of HBM per device.

v0:
```python
import jax
import jax.numpy as jnp
from jax import lax
from jax.experimental import pallas as pl
from jax.experimental.pallas import tpu as pltpu
from jax.sharding import PartitionSpec as P


H = 10
HD = 256
WINDOW = 2048
TQ = 256
HPAIR = 5


def normalize(rows, gain):
    rows32 = rows.astype(jnp.float32)
    factor = lax.rsqrt(jnp.mean(rows32 * rows32, axis=-1, keepdims=True) + 1e-06)
    return (rows32 * factor * gain).astype(jnp.bfloat16)


def _attn_kernel(len_ref, q_ref, pk_ref, pv_ref, sk_ref, sv_ref, o_ref, s_ref, p_ref):
    n = len_ref[0]
    pre = pk_ref.shape[0]
    count = q_ref.shape[0]
    nt = (((1,), (1,)), ((), ()))
    for hh in range(q_ref.shape[1] // HD):
        for i in range(count // TQ):
            r0 = i * TQ
            c0 = hh * HD
            lp = pre - r0
            ns = r0 + TQ
            q = q_ref[r0:r0 + TQ, c0:c0 + HD] * jnp.asarray(HD ** (-0.5), q_ref.dtype)
            qpos = r0 + lax.broadcasted_iota(jnp.int32, (TQ, 1), 0)
            s_ref[:, :lp] = lax.dot_general(q, pk_ref[r0:, :], nt, preferred_element_type=jnp.float32)
            s_ref[:, lp:lp + ns] = lax.dot_general(q, sk_ref[:ns, :], nt, preferred_element_type=jnp.float32)
            ppos = r0 + lax.broadcasted_iota(jnp.int32, (1, TQ), 1)
            vis_p = (ppos > pre + qpos - WINDOW) & (ppos <= pre + qpos) & (ppos < pre + n)
            s_ref[:, :TQ] = jnp.where(vis_p, s_ref[:, :TQ], -1e30)
            spos = pre + lax.broadcasted_iota(jnp.int32, (1, ns), 1)
            vis_s = (spos > pre + qpos - WINDOW) & (spos <= pre + qpos) & (spos < pre + n)
            s_ref[:, lp:lp + ns] = jnp.where(vis_s, s_ref[:, lp:lp + ns], -1e30)
            s = s_ref[:, :lp + ns]
            top = jnp.max(s, axis=-1, keepdims=True)
            e = jnp.exp(s - top)
            s_ref[...] = e
            inv = 1.0 / jnp.sum(e, axis=-1, keepdims=True)
            p_ref[...] = (s_ref[...] * inv).astype(p_ref.dtype)
            acc = jnp.dot(p_ref[:, :lp], pv_ref[r0:, :], preferred_element_type=jnp.float32)
            out = acc + jnp.dot(p_ref[:, lp:lp + ns], sv_ref[:ns, :], preferred_element_type=jnp.float32)
            o_ref[r0:r0 + TQ, c0:c0 + HD] = jnp.where(qpos < n, out, 0.0).astype(o_ref.dtype)


def attend(qkv, prefix, length):
    count = qkv.shape[0]
    pre = prefix.shape[0]
    width = pre + TQ
    grid_spec = pltpu.PrefetchScalarGridSpec(
        num_scalar_prefetch=1,
        grid=(H // HPAIR,),
        in_specs=[
            pl.BlockSpec((count, HPAIR * HD), lambda h, n: (0, h)),
            pl.BlockSpec((pre, HD), lambda h, n: (0, 0)),
            pl.BlockSpec((pre, HD), lambda h, n: (0, 1)),
            pl.BlockSpec((count, HD), lambda h, n: (0, H)),
            pl.BlockSpec((count, HD), lambda h, n: (0, H + 1)),
        ],
        out_specs=pl.BlockSpec((count, HPAIR * HD), lambda h, n: (0, h)),
        scratch_shapes=[
            pltpu.VMEM((TQ, width), jnp.float32),
            pltpu.VMEM((TQ, width), jnp.bfloat16),
        ],
    )
    flops = 4 * H * count * width * HD
    return pl.pallas_call(
        _attn_kernel,
        out_shape=jax.ShapeDtypeStruct((count, H * HD), jnp.bfloat16),
        grid_spec=grid_spec,
        compiler_params=pltpu.CompilerParams(vmem_limit_bytes=48 * 1024 * 1024),
        cost_estimate=pl.CostEstimate(
            flops=flops,
            transcendentals=H * count * width,
            bytes_accessed=2 * (count * qkv.shape[1] + pre * prefix.shape[1] + count * H * HD),
        ),
    )(length.reshape(1).astype(jnp.int32), qkv, prefix, prefix, qkv, qkv)


def gather_by_a2a(piece, axis_name, count):
    spread = jnp.broadcast_to(piece[None], (count,) + piece.shape)
    return lax.all_to_all(spread, axis_name, 0, 0, tiled=True)


def shards(tokens, gain, w_qkv, prefix_kv, prefix_owner, suffix_len, slots):
    tok_dev = tokens.shape[0]
    n_grp = lax.axis_size("grp")
    n_shard = lax.axis_size("shard")
    core = lax.axis_index("grp") % 2
    pairs = [(g, g ^ 1) for g in range(n_grp)]

    owner = prefix_owner[0]
    sliced = gather_by_a2a(prefix_kv[0], "grp", n_grp)
    chosen = lax.dynamic_index_in_dim(sliced, owner, 0, keepdims=False)
    prefix = gather_by_a2a(chosen, "shard", n_shard).reshape(-1, chosen.shape[-1])

    here = slots.reshape(tok_dev, 1) % tok_dev
    code = jnp.concatenate([here // 32, here % 32], axis=1).astype(tokens.dtype)
    code = jnp.pad(code, ((0, 0), (0, 126)))
    sent = jnp.concatenate([tokens, code], axis=1)
    prefix, sent = lax.optimization_barrier((prefix, sent))
    arrived = lax.all_to_all(sent, "shard", 0, 0, tiled=True)
    d = tokens.shape[1]
    pos = arrived[:, d].astype(jnp.int32) * 32 + arrived[:, d + 1].astype(jnp.int32)
    onehot = (jnp.arange(tok_dev, dtype=jnp.int32)[:, None] == pos[None, :]).astype(jnp.bfloat16)
    placed = jnp.dot(onehot, arrived, preferred_element_type=jnp.float32).astype(jnp.bfloat16)[:, :d]
    normed = normalize(placed, gain)

    d = w_qkv.shape[0]
    kh = d // 2
    w_mine = lax.dynamic_slice_in_dim(w_qkv, core * kh, kh, axis=0)
    w_rows = lax.all_gather(w_mine, "shard", axis=1, tiled=True)
    w_other = lax.ppermute(w_rows, "grp", pairs)
    n_mine = lax.dynamic_slice_in_dim(normed, core * kh, kh, axis=1)
    n_other = lax.dynamic_slice_in_dim(normed, (1 - core) * kh, kh, axis=1)
    acc = jnp.dot(n_mine, w_rows, preferred_element_type=jnp.float32)
    acc = acc + jnp.dot(n_other, w_other, preferred_element_type=jnp.float32)
    qkv = acc.astype(jnp.bfloat16)

    lengths = suffix_len.reshape(-1)
    return attend(qkv, prefix, lengths[0])


def solution(mesh):
    return jax.shard_map(
        shards,
        mesh=mesh,
        in_specs=(
            P(("grp", "shard"), None),
            P(),
            P(None, "shard"),
            P("grp", "shard", None),
            P("grp"),
            P("grp", "shard"),
            P("grp", "shard"),
        ),
        out_specs=P(("grp", "shard"), None),
        check_vma=False,
    )
```

profile of v0, /device:TPU:0, one launch (start us, length us, event | category | flops | bytes accessed | tf_op | source)
XLA Modules:
  0.0 218.5 jit_solution(12975732720819782162)
XLA Ops:
  6.5 0.0 copy-start
  6.5 0.0 all-gather.2.cloned.1.call-start
  6.5 1.2 copy-done
  7.7 0.8 constant_dynamic-slice_fusion
  8.6 0.0 all-gather.2.cloned.1.call-update
  8.6 2.0 broadcast_in_dim.9
  10.6 4.6 %all-to-all-start = ((bf16[8,128,512]{2,1,0:T(8,128)(2,1)}), bf16[8,128,512]{2,1,0:T(8,128)(2,1)S(1)}, u32[]{:S(2)}, u32[]{:S(2)}) async-start(bf16[8,128,512]{2,1,0:T(8,128)(2,1)} %broadcast_in_dim.9), calls=%async_computation | async-start | bytes 2097152 | tf_op jit(solution)/shard_map/all_to_all | solution.py:90
  15.2 65.5 %all-gather.2.cloned.1.call-done = bf16[1280,3072]{0,1:T(8,128)(2,1)} async-done(((bf16[1280,192]{0,1:T(8,128)(2,1)}), bf16[1280,3072]{0,1:T(8,128)(2,1)}) %all-gather.2.cloned.1.call-update) | async-done | bytes 7864336 | tf_op jit(solution)/shard_map/all_gather | solution.py:120
  80.6 0.0 collective-permute-start
  81.3 0.0 all-to-all-done
  81.3 0.0 copy-start.2
  81.3 1.5 broadcast_in_dim.22
  82.9 5.3 %all-to-all-start.1 = ((bf16[16,128,512]{2,1,0:T(8,128)(2,1)}), bf16[16,128,512]{2,1,0:T(8,128)(2,1)S(1)}, u32[]{:S(2)}, u32[]{:S(2)}) async-start(bf16[16,128,512]{2,1,0:T(8,128)(2,1)} %broadcast_in_dim.22), calls=%async_computation.1 | async-start | bytes 4194304 | tf_op jit(solution)/shard_map/all_to_all | solution.py:90
  88.1 0.0 copy-done.2
  88.2 0.2 copy.15
  88.4 3.5 %fusion.4 = bf16[512,2688]{1,0:T(8,128)(2,1)} fusion(bf16[512,2]{1,0:T(8,128)(2,1)S(1)} %copy.15, bf16[512,2560]{1,0:T(8,128)(2,1)} %param.7), kind=kLoop, calls=%fused_computation.9 | loop fusion | flops 8257536 | bytes 5376000 | tf_op jit(solution)/shard_map/concatenate | solution.py:108
  91.8 30.4 %all-to-all-done.1 = bf16[16,128,512]{2,1,0:T(8,128)(2,1)S(1)} async-done(((bf16[16,128,512]{2,1,0:T(8,128)(2,1)}), bf16[16,128,512]{2,1,0:T(8,128)(2,1)S(1)}, u32[]{:S(2)}, u32[]{:S(2)}) %all-to-all-start.1) | async-done | bytes 2097184 | tf_op jit(solution)/shard_map/all_to_all | solution.py:90
  122.3 4.5 %all-to-all-start.2 = ((bf16[16,32,2688]{2,1,0:T(8,128)(2,1)}), bf16[16,32,2688]{2,1,0:T(8,128)(2,1)}, u32[]{:S(2)}, u32[]{:S(2)}) async-start(bf16[16,32,2688]{2,1,0:T(8,128)(2,1)} %bitcast.20), calls=%async_computation.2 | async-start | bytes 5505024 | tf_op jit(solution)/shard_map/all_to_all | solution.py:110
  127.4 40.6 %all-to-all-done.2 = bf16[16,32,2688]{2,1,0:T(8,128)(2,1)} async-done(((bf16[16,32,2688]{2,1,0:T(8,128)(2,1)}), bf16[16,32,2688]{2,1,0:T(8,128)(2,1)}, u32[]{:S(2)}, u32[]{:S(2)}) %all-to-all-start.2) | async-done | bytes 2752544 | tf_op jit(solution)/shard_map/all_to_all | solution.py:110
  168.1 1.1 fusion.15
  169.2 0.1 copy.13
  169.3 0.1 copy.14
  169.4 0.0 copy-start.1
  169.4 0.0 slice-start
  169.4 3.6 %fusion.8 = bf16[512,2688]{1,0:T(8,128)(2,1)S(1)} fusion(bf16[512,2688]{1,0:T(8,128)(2,1)} %bitcast.7, s32[512]{0:T(512)S(1)} %bitcast.22), kind=kOutput, calls=%fused_computation.14 | convolution fusion | flops 1409548288 | bytes 5507072 | tf_op jit(solution)/shard_map/dot_general | solution.py:114
  173.0 0.0 slice-start.1
  173.1 0.6 fusion.1
  173.6 0.0 copy-done.1
  173.7 0.7 fusion.3
  174.3 0.0 slice-done
  174.3 0.7 slice-done.1
  175.1 6.1 %fusion.6 = f32[512,3072]{1,0:T(8,128)} fusion(bf16[1280,3072]{0,1:T(8,128)(2,1)S(1)} %bitcast.24, bf16[512,2560]{1,0:T(8,128)(2,1)S(1)} %fusion.3, s32[]{:T(128)S(6)} %select_n.66), kind=kOutput, calls=%fused_computation.11 | convolution fusion | flops 4026531840 | bytes 15466500 | tf_op jit(solution)/shard_map/dot_general | solution.py:124
  181.2 0.0 collective-permute-done
  181.2 8.8 %add_convert_fusion.q_ref.sk_ref.sv_ref = bf16[512,3072]{1,0:T(8,128)(2,1)S(1)} fusion(f32[512,3072]{1,0:T(8,128)} %fusion.6, bf16[1280,3072]{0,1:T(8,128)(2,1)} %collective-permute-done, bf16[512,2560]{1,0:T(8,128)(2,1)S(1)} %fusion.3, s32[]{:T(128)S(6)} %select_n.67), kind=kOutput, calls=%fused_computation.2 | convolution fusion | flops 4029677568 | bytes 18612228 | tf_op jit(solution)/shard_map/dot_general | solution.py:125
  190.0 21.6 %shard_map.73 = bf16[512,2560]{1,0:T(8,128)(2,1)} custom-call(s32[1]{0:T(128)} %bitcast.17.len_ref, bf16[512,3072]{1,0:T(8,128)(2,1)S(1)} %add_convert_fusion.q_ref.sk_ref.sv_ref, bf16[2048,512]{1,0:T(8,128)(2,1)S(1)} %bitcast.18, bf16[2048,512]{1,0:T(8,128)(2,1)S(1)} %bitcast.19, bf16[512,3072]{1,0:T(8,128)(2,1)S(1)} %add_convert_fusion.q_ref.sk_ref.sv_ref, ...), custom_call_target="tpu_custom_call" | custom-call | flops 12079595520 | bytes 7864320 | tf_op jit(solution)/shard_map/pallas_call | solution.py:75
  (7 shorter events, 0.1 us)
Async XLA Ops:
  6.5 1.2 copy-start
  6.5 74.1 %all-gather.2.cloned.1.call-start = ((), (), s32[]{:S(2)}) async-start(), calls=%async_computation.3 | async-start | bytes 8355840 | tf_op jit(solution)/shard_map/all_gather | solution.py:120
  10.6 70.7 %all-to-all-start = ((bf16[8,128,512]{2,1,0:T(8,128)(2,1)}), bf16[8,128,512]{2,1,0:T(8,128)(2,1)S(1)}, u32[]{:S(2)}, u32[]{:S(2)}) async-start(bf16[8,128,512]{2,1,0:T(8,128)(2,1)} %broadcast_in_dim.9), calls=%async_computation | async-start | bytes 2097152 | tf_op jit(solution)/shard_map/all_to_all | solution.py:90
  80.6 100.6 %collective-permute-start = (bf16[1280,3072]{0,1:T(8,128)(2,1)}, bf16[1280,3072]{0,1:T(8,128)(2,1)}, u32[]{:S(2)}, u32[]{:S(2)}) collective-permute-start(bf16[1280,3072]{0,1:T(8,128)(2,1)} %all-gather.2.cloned.1.call-done), channel_id=1, source_target_pairs={{0,16},{16,0},{32,48},{48,32},{64,80},{80,64},{96,112},{112,96},{1... | collective-permute-start | bytes 23592968 | tf_op jit(solution)/shard_map/ppermute | solution.py:121
  81.3 6.8 %copy-start.2 = (s32[1,512]{1,0:T(1,128)S(1)}, s32[1,512]{1,0:T(1,128)}, u32[]{:S(2)}) copy-start(s32[1,512]{1,0:T(1,128)} %param.13) | copy-start | bytes 6148
  82.9 39.4 %all-to-all-start.1 = ((bf16[16,128,512]{2,1,0:T(8,128)(2,1)}), bf16[16,128,512]{2,1,0:T(8,128)(2,1)S(1)}, u32[]{:S(2)}, u32[]{:S(2)}) async-start(bf16[16,128,512]{2,1,0:T(8,128)(2,1)} %broadcast_in_dim.22), calls=%async_computation.1 | async-start | bytes 4194304 | tf_op jit(solution)/shard_map/all_to_all | solution.py:90
  122.3 45.8 %all-to-all-start.2 = ((bf16[16,32,2688]{2,1,0:T(8,128)(2,1)}), bf16[16,32,2688]{2,1,0:T(8,128)(2,1)}, u32[]{:S(2)}, u32[]{:S(2)}) async-start(bf16[16,32,2688]{2,1,0:T(8,128)(2,1)} %bitcast.20), calls=%async_computation.2 | async-start | bytes 5505024 | tf_op jit(solution)/shard_map/all_to_all | solution.py:110
  169.4 4.2 %copy-start.1 = (f32[2560]{0:T(1024)S(1)}, f32[2560]{0:T(1024)}, u32[]{:S(2)}) copy-start(f32[2560]{0:T(1024)} %param.8) | copy-start | bytes 30724
  169.4 4.9 %slice-start = ((s8[7864320]{0:T(1024)(128)(4,1)}), s8[4194304]{0:T(1024)(128)(4,1)S(1)}, s32[]{:S(2)}) async-start(s8[7864320]{0:T(1024)(128)(4,1)} %bitcast.23), calls=%async_computation.4 | async-start | bytes 8388608
  173.0 2.0 slice-start.1
Sparse Core Ops, SparseCore 0:
  9.5 71.1 all-gather.1
where the time goes:
time: 219 us; the launch traced here: 218 us
  waiting for transfers between devices  137 us (63%)
  Pallas kernels  21.6 us (10%)
  matrix products  18.5 us (8%)
  between operations  14.9 us (7%)
  starting transfers between devices  14.3 us (7%)
  local copies, waits for them, and re-layouts  7.8 us (4%)
  other arithmetic  4.76 us (2%)
    all_gather x1, waiting for transfers between devices, shards(): w_rows = lax.all_gather(w_mine, 'shard', axis=1, tiled=True)  65.5 us
    all_to_all x1, waiting for transfers between devices, shards(): arrived = lax.all_to_all(sent, 'shard', 0, 0, tiled=True)  40.6 us
    all_to_all x2, waiting for transfers between devices, gather_by_a2a(): return lax.all_to_all(spread, axis_name, 0, 0, tiled=True)  30.4 us
    pallas_call x1, Pallas kernels, attend(): pl.pallas_call(_attn_kernel, out_shape=jax.ShapeDtypeStruct((count, H * H...  21.6 us
    all_to_all x2, starting transfers between devices, gather_by_a2a(): return lax.all_to_all(spread, axis_name, 0, 0, tiled=True)  9.84 us
    dot_general x1, matrix products, shards(): acc = acc + jnp.dot(n_other, w_other, preferred_element_type=jnp.float32)  8.76 us
    dot_general x1, matrix products, shards(): acc = jnp.dot(n_mine, w_rows, preferred_element_type=jnp.float32)  6.11 us
    all_to_all x1, starting transfers between devices, shards(): arrived = lax.all_to_all(sent, 'shard', 0, 0, tiled=True)  4.49 us
  transfers between devices with their start and end apart: 5, of which 3 were waited for; matrix products, arithmetic and copies ran while one was open for 9% of the time, Pallas kernels for 0%

commit v1 on v0

--- a/solution.py
+++ b/solution.py
@@ -10,7 +10,7 @@
 HD = 256
 WINDOW = 2048
 TQ = 256
-HPAIR = 5
+HPAIR = 10
 
 
 def normalize(rows, gain):
@@ -43,9 +43,8 @@
             s = s_ref[:, :lp + ns]
             top = jnp.max(s, axis=-1, keepdims=True)
             e = jnp.exp(s - top)
-            s_ref[...] = e
             inv = 1.0 / jnp.sum(e, axis=-1, keepdims=True)
-            p_ref[...] = (s_ref[...] * inv).astype(p_ref.dtype)
+            p_ref[...] = (e * inv).astype(p_ref.dtype)
             acc = jnp.dot(p_ref[:, :lp], pv_ref[r0:, :], preferred_element_type=jnp.float32)
             out = acc + jnp.dot(p_ref[:, lp:lp + ns], sv_ref[:ns, :], preferred_element_type=jnp.float32)
             o_ref[r0:r0 + TQ, c0:c0 + HD] = jnp.where(qpos < n, out, 0.0).astype(o_ref.dtype)
@@ -105,9 +104,7 @@
     here = slots.reshape(tok_dev, 1) % tok_dev
     code = jnp.concatenate([here // 32, here % 32], axis=1).astype(tokens.dtype)
     code = jnp.pad(code, ((0, 0), (0, 126)))
-    sent = jnp.concatenate([tokens, code], axis=1)
-    prefix, sent = lax.optimization_barrier((prefix, sent))
-    arrived = lax.all_to_all(sent, "shard", 0, 0, tiled=True)
+    arrived = lax.all_to_all(jnp.concatenate([tokens, code], axis=1), "shard", 0, 0, tiled=True)
     d = tokens.shape[1]
     pos = arrived[:, d].astype(jnp.int32) * 32 + arrived[:, d + 1].astype(jnp.int32)
     onehot = (jnp.arange(tok_dev, dtype=jnp.int32)[:, None] == pos[None, :]).astype(jnp.bfloat16)

time: 219 us -> 214 us (0.977)
  waiting for transfers between devices: 137 us -> 131 us
    all_to_all x2, waiting for transfers between devices: 30.4 us -> 18.7 us  [gather_by_a2a(): return lax.all_to_all(spread, axis_name, 0, 0, tiled=True)]
    all_gather x1, waiting for transfers between devices: 65.5 us -> 72.1 us  [shards(): w_rows = lax.all_gather(w_mine, 'shard', axis=1, tiled=True)]
  transfers between devices with their start and end apart: 5 -> 5, of which waited for: 3 -> 4; matrix products, arithmetic and copies ran while one was open for 9% -> 14% of each run, Pallas kernels for 0% -> 0%
where the time goes in v1:
time: 214 us; the launch traced here: 213 us
  waiting for transfers between devices  131 us (61%)
  Pallas kernels  20.3 us (9%)
  matrix products  19.6 us (9%)
  between operations  14.8 us (7%)
  starting transfers between devices  13.4 us (6%)
  local copies, waits for them, and re-layouts  9.65 us (5%)
  other arithmetic  4.76 us (2%)
    all_gather x1, waiting for transfers between devices, shards(): w_rows = lax.all_gather(w_mine, 'shard', axis=1, tiled=True)  72.1 us
    all_to_all x1, waiting for transfers between devices, shards(): lax.all_to_all(jnp.concatenate([tokens, code], axis=1), 'shard', 0, 0, ti...  39.8 us
    pallas_call x1, Pallas kernels, attend(): pl.pallas_call(_attn_kernel, out_shape=jax.ShapeDtypeStruct((count, H * H...  20.3 us
    all_to_all x2, waiting for transfers between devices, gather_by_a2a(): return lax.all_to_all(spread, axis_name, 0, 0, tiled=True)  18.7 us
    dot_general x1, matrix products, shards(): acc = acc + jnp.dot(n_other, w_other, preferred_element_type=jnp.float32)  9.88 us
    all_to_all x2, starting transfers between devices, gather_by_a2a(): return lax.all_to_all(spread, axis_name, 0, 0, tiled=True)  8.12 us
    dot_general x1, matrix products, shards(): acc = jnp.dot(n_mine, w_rows, preferred_element_type=jnp.float32)  6.13 us
    all_to_all x1, starting transfers between devices, shards(): lax.all_to_all(jnp.concatenate([tokens, code], axis=1), 'shard', 0, 0, ti...  5.3 us
  transfers between devices with their start and end apart: 5, of which 4 were waited for; matrix products, arithmetic and copies ran while one was open for 14% of the time, Pallas kernels for 0%

profile of v1, /device:TPU:0, one launch (start us, length us, event | category | flops | bytes accessed | tf_op | source)
XLA Modules:
  0.0 213.1 jit_solution(10216109433515007863)
XLA Ops:
  6.5 0.0 copy-start
  6.5 0.0 copy-start.3
  6.5 0.0 all-gather.2.cloned.1.call-start
  6.5 1.2 copy-done
  7.7 0.8 constant_dynamic-slice_fusion
  8.5 0.0 all-gather.2.cloned.1.call-update
  8.6 72.1 %all-gather.2.cloned.1.call-done = bf16[1280,3072]{0,1:T(8,128)(2,1)} async-done(((bf16[1280,192]{0,1:T(8,128)(2,1)}), bf16[1280,3072]{0,1:T(8,128)(2,1)}) %all-gather.2.cloned.1.call-update) | async-done | bytes 7864336 | tf_op jit(solution)/shard_map/all_gather | solution.py:117
  80.6 0.0 collective-permute-start
  80.6 2.0 broadcast_in_dim.9
  82.6 4.4 %all-to-all-start.1 = ((bf16[8,128,512]{2,1,0:T(8,128)(2,1)}), bf16[8,128,512]{2,1,0:T(8,128)(2,1)S(1)}, u32[]{:S(2)}, u32[]{:S(2)}) async-start(bf16[8,128,512]{2,1,0:T(8,128)(2,1)} %broadcast_in_dim.9), calls=%async_computation.1 | async-start | bytes 2097152 | tf_op jit(solution)/shard_map/all_to_all | solution.py:89
  87.0 0.0 copy-done.3
  87.1 0.2 copy.15
  87.3 3.5 %fusion.4 = bf16[512,2688]{1,0:T(8,128)(2,1)} fusion(bf16[512,2]{1,0:T(8,128)(2,1)S(1)} %copy.15, bf16[512,2560]{1,0:T(8,128)(2,1)} %param.7), kind=kLoop, calls=%fused_computation.9 | loop fusion | flops 8257536 | bytes 5376000 | tf_op jit(solution)/shard_map/concatenate | solution.py:107
  90.7 12.2 %all-to-all-done.1 = bf16[8,128,512]{2,1,0:T(8,128)(2,1)S(1)} async-done(((bf16[8,128,512]{2,1,0:T(8,128)(2,1)}), bf16[8,128,512]{2,1,0:T(8,128)(2,1)S(1)}, u32[]{:S(2)}, u32[]{:S(2)}) %all-to-all-start.1) | async-done | bytes 1048608 | tf_op jit(solution)/shard_map/all_to_all | solution.py:89
  102.9 5.3 %all-to-all-start = ((bf16[16,32,2688]{2,1,0:T(8,128)(2,1)}), bf16[16,32,2688]{2,1,0:T(8,128)(2,1)}, u32[]{:S(2)}, u32[]{:S(2)}) async-start(bf16[16,32,2688]{2,1,0:T(8,128)(2,1)} %bitcast.20), calls=%async_computation | async-start | bytes 5505024 | tf_op jit(solution)/shard_map/all_to_all | solution.py:107
  109.6 39.8 %all-to-all-done = bf16[16,32,2688]{2,1,0:T(8,128)(2,1)} async-done(((bf16[16,32,2688]{2,1,0:T(8,128)(2,1)}), bf16[16,32,2688]{2,1,0:T(8,128)(2,1)}, u32[]{:S(2)}, u32[]{:S(2)}) %all-to-all-start) | async-done | bytes 2752544 | tf_op jit(solution)/shard_map/all_to_all | solution.py:107
  149.3 1.5 broadcast_in_dim.22
  150.9 3.7 %all-to-all-start.2 = ((bf16[16,128,512]{2,1,0:T(8,128)(2,1)}), bf16[16,128,512]{2,1,0:T(8,128)(2,1)S(1)}, u32[]{:S(2)}, u32[]{:S(2)}) async-start(bf16[16,128,512]{2,1,0:T(8,128)(2,1)} %broadcast_in_dim.22), calls=%async_computation.2 | async-start | bytes 4194304 | tf_op jit(solution)/shard_map/all_to_all | solution.py:89
  154.6 1.1 fusion.15
  155.7 0.1 copy.13
  155.8 0.1 copy.14
  155.9 0.0 copy-start.2
  155.9 0.0 slice-start
  156.0 3.6 %fusion.8 = bf16[512,2688]{1,0:T(8,128)(2,1)S(1)} fusion(bf16[512,2688]{1,0:T(8,128)(2,1)} %bitcast.3, s32[512]{0:T(512)S(1)} %bitcast.22), kind=kOutput, calls=%fused_computation.14 | convolution fusion | flops 1409548288 | bytes 5507072 | tf_op jit(solution)/shard_map/dot_general | solution.py:111
  159.6 0.0 slice-start.1
  159.6 0.6 fusion.1
  160.2 0.0 copy-done.2
  160.2 0.7 fusion.3
  160.8 0.0 slice-done
  160.9 0.7 slice-done.1
  161.6 6.1 %fusion.6 = f32[512,3072]{1,0:T(8,128)} fusion(bf16[1280,3072]{0,1:T(8,128)(2,1)S(1)} %bitcast.24, bf16[512,2560]{1,0:T(8,128)(2,1)S(1)} %fusion.3, s32[]{:T(128)S(6)} %select_n.65), kind=kOutput, calls=%fused_computation.11 | convolution fusion | flops 4026531840 | bytes 15466500 | tf_op jit(solution)/shard_map/dot_general | solution.py:121
  167.7 0.0 collective-permute-done
  167.7 9.9 %add_convert_fusion.q_ref.sk_ref.sv_ref = bf16[512,3072]{1,0:T(8,128)(2,1)} fusion(f32[512,3072]{1,0:T(8,128)} %fusion.6, bf16[1280,3072]{0,1:T(8,128)(2,1)} %collective-permute-done, bf16[512,2560]{1,0:T(8,128)(2,1)S(1)} %fusion.3, s32[]{:T(128)S(6)} %select_n.66), kind=kOutput, calls=%fused_computation.2 | convolution fusion | flops 4029677568 | bytes 18612228 | tf_op jit(solution)/shard_map/dot_general | solution.py:122
  177.6 6.5 %all-to-all-done.2 = bf16[16,128,512]{2,1,0:T(8,128)(2,1)S(1)} async-done(((bf16[16,128,512]{2,1,0:T(8,128)(2,1)}), bf16[16,128,512]{2,1,0:T(8,128)(2,1)S(1)}, u32[]{:S(2)}, u32[]{:S(2)}) %all-to-all-start.2) | async-done | bytes 2097184 | tf_op jit(solution)/shard_map/all_to_all | solution.py:89
  184.1 0.0 copy-start.1
  184.1 1.9 copy-done.1
  186.0 20.3 %shard_map.73 = bf16[512,2560]{1,0:T(8,128)(2,1)} custom-call(s32[1]{0:T(128)} %bitcast.17.len_ref, bf16[512,3072]{1,0:T(8,128)(2,1)S(1)} %copy-done.1, bf16[2048,512]{1,0:T(8,128)(2,1)S(1)} %bitcast.18, bf16[2048,512]{1,0:T(8,128)(2,1)S(1)} %bitcast.19, bf16[512,3072]{1,0:T(8,128)(2,1)S(1)} %copy-done.1, bf16[512,3072]{1,0:T(8,128)(2,1)S(1)} %copy-done.1), custom_call_target="tpu_custom_call" | custom-call | flops 12079595520 | bytes 7864320 | tf_op jit(solution)/shard_map/pallas_call | solution.py:74
  (7 shorter events, 0.1 us)
Async XLA Ops:
  6.5 1.2 copy-start
  6.5 80.5 %copy-start.3 = (s32[1,512]{1,0:T(1,128)S(1)}, s32[1,512]{1,0:T(1,128)}, u32[]{:S(2)}) copy-start(s32[1,512]{1,0:T(1,128)} %param.13) | copy-start | bytes 6148
  6.5 74.1 %all-gather.2.cloned.1.call-start = ((), (), s32[]{:S(2)}) async-start(), calls=%async_computation.3 | async-start | bytes 8355840 | tf_op jit(solution)/shard_map/all_gather | solution.py:117
  80.6 87.1 %collective-permute-start = (bf16[1280,3072]{0,1:T(8,128)(2,1)}, bf16[1280,3072]{0,1:T(8,128)(2,1)}, u32[]{:S(2)}, u32[]{:S(2)}) collective-permute-start(bf16[1280,3072]{0,1:T(8,128)(2,1)} %all-gather.2.cloned.1.call-done), channel_id=1, source_target_pairs={{0,16},{16,0},{32,48},{48,32},{64,80},{80,64},{96,112},{112,96},{1... | collective-permute-start | bytes 23592968 | tf_op jit(solution)/shard_map/ppermute | solution.py:118
  82.6 20.3 %all-to-all-start.1 = ((bf16[8,128,512]{2,1,0:T(8,128)(2,1)}), bf16[8,128,512]{2,1,0:T(8,128)(2,1)S(1)}, u32[]{:S(2)}, u32[]{:S(2)}) async-start(bf16[8,128,512]{2,1,0:T(8,128)(2,1)} %broadcast_in_dim.9), calls=%async_computation.1 | async-start | bytes 2097152 | tf_op jit(solution)/shard_map/all_to_all | solution.py:89
  102.9 46.4 %all-to-all-start = ((bf16[16,32,2688]{2,1,0:T(8,128)(2,1)}), bf16[16,32,2688]{2,1,0:T(8,128)(2,1)}, u32[]{:S(2)}, u32[]{:S(2)}) async-start(bf16[16,32,2688]{2,1,0:T(8,128)(2,1)} %bitcast.20), calls=%async_computation | async-start | bytes 5505024 | tf_op jit(solution)/shard_map/all_to_all | solution.py:107
  150.9 33.2 %all-to-all-start.2 = ((bf16[16,128,512]{2,1,0:T(8,128)(2,1)}), bf16[16,128,512]{2,1,0:T(8,128)(2,1)S(1)}, u32[]{:S(2)}, u32[]{:S(2)}) async-start(bf16[16,128,512]{2,1,0:T(8,128)(2,1)} %broadcast_in_dim.22), calls=%async_computation.2 | async-start | bytes 4194304 | tf_op jit(solution)/shard_map/all_to_all | solution.py:89
  155.9 4.2 %copy-start.2 = (f32[2560]{0:T(1024)S(1)}, f32[2560]{0:T(1024)}, u32[]{:S(2)}) copy-start(f32[2560]{0:T(1024)} %param.8) | copy-start | bytes 30724
  155.9 4.9 %slice-start = ((s8[7864320]{0:T(1024)(128)(4,1)}), s8[4194304]{0:T(1024)(128)(4,1)S(1)}, s32[]{:S(2)}) async-start(s8[7864320]{0:T(1024)(128)(4,1)} %bitcast.23), calls=%async_computation.4 | async-start | bytes 8388608
  159.6 2.0 slice-start.1
  184.1 1.9 copy-start.1
Sparse Core Ops, SparseCore 0:
  9.5 71.1 all-gather.1
